TPU v7x, 32 devices: a whole 2x2x4 slice. The times are simulated.
32 devices in a mesh: lat: 8 (over y, x, core), lon: 4 (over z).
Axes of the slice: x: 2, y: 2, z: 4, core: 2. Of those that a mesh axis runs over, the one named last changes fastest.
Arguments:
- tracers: float32 [5, 4, 64, 2880], P(None, None, 'lat', 'lon'), may hold values from -6 to 6
- courant_x: float32 [4, 64, 2880], P(None, 'lat', 'lon'), may hold values from -0.3 to 0.3
- courant_y: float32 [4, 64, 2880], P(None, 'lat', 'lon'), may hold values from -0.3 to 0.3
- cutoffs: int32 [64], replicated, may hold values from 1 to 720, as said below
Outputs:
- advected: float32 [5, 4, 64, 2880], P(None, None, 'lat', 'lon')
Inputs may be any that keep to these rules, and one draw needn't show every extreme that they name: `cutoffs`: some row poleward of 45 degrees keeps exactly 720 wavenumbers.
All inputs are finite; a program needn't handle non-finite values.
Results may differ from a plain program's by a relative error of at most 0.0003.
Values sent between devices are 32-bit elements; how exact they have to be, the bound alone decides.
No kernel may reach another device: no remote copies, remote signals or barrier semaphores. Data moves between devices by JAX's collectives and lax.ppermute only.
A program may use at most 64 MiB of HBM per device.

v0:
```python
import math
import jax
import jax.numpy as jnp
from jax import lax
from jax.sharding import PartitionSpec as P

KMAX = 720
SUBSTEPS = 2


def extended_2(cells, sides, width):
    for axis, dim in sides:
        count = lax.axis_size(axis)
        head = lax.slice_in_dim(cells, 0, width, axis=dim)
        tail = lax.slice_in_dim(cells, cells.shape[dim] - width, cells.shape[dim], axis=dim)
        cells = jnp.concatenate(
            [
                lax.ppermute(tail, axis, [(i, (i + 1) % count) for i in range(count)]),
                cells,
                lax.ppermute(head, axis, [((i + 1) % count, i) for i in range(count)]),
            ],
            axis=dim,
        )
    return cells


def from_behind(x, axis, by):
    size = lax.axis_size(axis)
    return lax.ppermute(x, axis, [(i, (i + by) % size) for i in range(size)])


def window(values, first_cell, last_cell, dim_at):
    return lax.slice_in_dim(values, first_cell, last_cell, axis=dim_at)


def ppm_flux(padded, courant, dim_at, cell_count):
    edge_values = 7.0 / 12.0 * (
        window(padded, 1, cell_count + 4, dim_at) + window(padded, 2, cell_count + 5, dim_at)
    ) - 1.0 / 12.0 * (
        window(padded, 0, cell_count + 3, dim_at) + window(padded, 3, cell_count + 6, dim_at)
    )
    left_edge = window(edge_values, 0, cell_count + 1, dim_at)
    mid_edge = window(edge_values, 1, cell_count + 2, dim_at)
    right_edge = window(edge_values, 2, cell_count + 3, dim_at)
    left_cell = window(padded, 2, cell_count + 3, dim_at)
    right_cell = window(padded, 3, cell_count + 4, dim_at)
    magnitude = jnp.abs(courant)
    six_left = 6.0 * left_cell - 3.0 * (left_edge + mid_edge)
    six_right = 6.0 * right_cell - 3.0 * (mid_edge + right_edge)
    from_left = mid_edge - 0.5 * magnitude * (
        mid_edge - left_edge - (1.0 - magnitude * (2.0 / 3.0)) * six_left
    )
    from_right = mid_edge + 0.5 * magnitude * (
        right_edge - mid_edge + (1.0 - magnitude * (2.0 / 3.0)) * six_right
    )
    return courant * jnp.where(courant >= 0.0, from_left, from_right)


def dft_basis(first_col, column_count, circle):
    position = first_col + jnp.arange(column_count, dtype=jnp.int32)
    wavenumber = jnp.arange(KMAX, dtype=jnp.int32)
    phase_index = position[:, None] * wavenumber[None, :] % circle
    phase_angle = phase_index.astype(jnp.float32) * (2.0 * math.pi / circle)
    return jnp.concatenate([jnp.cos(phase_angle), jnp.sin(phase_angle)], axis=1)


def mode_weights(cut_rows, circle):
    wavenumber = jnp.arange(KMAX, dtype=jnp.int32)
    mode_scale = jnp.where(wavenumber == 0, 1.0 / circle, 2.0 / circle).astype(jnp.float32)
    weights = jnp.where(wavenumber[None, :] < cut_rows[:, None], mode_scale[None, :], 0.0)
    return jnp.concatenate([weights, weights], axis=1)


def on_device(tracers, courant_x, courant_y, cutoffs):
    tracer_count, level_count, lat_rows, lon_cols = tracers.shape
    field_count = tracer_count * level_count
    lat_devices = lax.axis_size("lat")
    lon_devices = lax.axis_size("lon")
    lat_index = lax.axis_index("lat")
    lon_index = lax.axis_index("lon")
    circle = lon_cols * lon_devices
    total_rows = lat_rows * lat_devices
    row_global = lat_index * lat_rows + jnp.arange(lat_rows, dtype=jnp.int32)
    face_global = lat_index * lat_rows + jnp.arange(lat_rows + 1, dtype=jnp.int32)
    face_angle = (face_global.astype(jnp.float32) / total_rows - 0.5) * math.pi
    face_weight = jnp.where(
        (face_global == 0) | (face_global == total_rows), 0.0, jnp.cos(face_angle)
    )
    center_weight = jnp.cos(((row_global.astype(jnp.float32) + 0.5) / total_rows - 0.5) * math.pi)
    polar_rows = (row_global < total_rows // 4) | (row_global >= total_rows - total_rows // 4)
    basis_tile = dft_basis(lon_index * lon_cols, lon_cols, circle)
    state = tracers
    for substep in range(SUBSTEPS):
        flat_rows = state.reshape(field_count, lat_rows, lon_cols)
        stacked = jnp.concatenate([flat_rows, courant_x, courant_y], axis=0)
        padded = extended_2(stacked, (("lat", 1), ("lon", 2)), 3)
        pad_tracer = padded[:field_count].reshape(
            tracer_count, level_count, lat_rows + 6, lon_cols + 6
        )
        pad_east = padded[field_count : field_count + level_count]
        pad_north = padded[field_count + level_count :]
        east_courant = pad_east[:, 3 : 3 + lat_rows, 2 : lon_cols + 3]
        zonal = ppm_flux(pad_tracer[:, :, 3 : 3 + lat_rows, :], east_courant, 3, lon_cols)
        edge_rows = jnp.concatenate([state[:, :, :3], state[:, :, lat_rows - 3 :]], axis=2)
        antipodal = from_behind(edge_rows, "lon", lon_devices // 2)
        south_rows = jnp.where(
            lat_index == 0, antipodal[:, :, 2::-1], pad_tracer[:, :, :3, 3 : 3 + lon_cols]
        )
        north_rows = jnp.where(
            lat_index == lat_devices - 1,
            antipodal[:, :, 5:2:-1],
            pad_tracer[:, :, lat_rows + 3 :, 3 : 3 + lon_cols],
        )
        extended = jnp.concatenate(
            [south_rows, pad_tracer[:, :, 3 : 3 + lat_rows, 3 : 3 + lon_cols], north_rows], axis=2
        )
        north_courant = pad_north[:, 3 : lat_rows + 4, 3 : 3 + lon_cols]
        meridional = ppm_flux(extended, north_courant, 2, lat_rows) * face_weight[:, None]
        change = (
            zonal[..., 1:]
            - zonal[..., :-1]
            + (meridional[:, :, 1:] - meridional[:, :, :-1]) / center_weight[:, None]
        )
        state = state - change
        flat_rows = state.reshape(field_count * lat_rows, lon_cols)
        band_cuts = lax.dynamic_slice_in_dim(cutoffs, lat_index * lat_rows, lat_rows)
        cut_rows = jnp.tile(band_cuts, field_count)
        partial_value = jnp.dot(flat_rows, basis_tile, precision=lax.Precision.HIGHEST)
        spectra = lax.psum(partial_value, "lon")
        weighted = spectra * mode_weights(cut_rows, circle)
        smooth = jnp.dot(weighted, basis_tile.T, precision=lax.Precision.HIGHEST)
        polar_flat = jnp.tile(polar_rows, field_count)
        filtered_rows = jnp.where(polar_flat[:, None], smooth, flat_rows)
        state = filtered_rows.reshape(tracer_count, level_count, lat_rows, lon_cols)
    return state


def solution(mesh):
    in_specs = (P(None, None, "lat", "lon"), P(None, "lat", "lon"), P(None, "lat", "lon"), P())
    out_specs = P(None, None, "lat", "lon")
    return jax.shard_map(
        on_device, mesh=mesh, in_specs=in_specs, out_specs=out_specs, check_vma=False
    )
```

profile of v0, /device:TPU:0, one launch (start us, length us, event | category | flops | bytes accessed | tf_op | source)
XLA Modules:
  0.0 247.9 jit_solution(7881026659669633347)
XLA Ops:
  6.5 1.3 fusion.126
  7.9 0.9 pad_maximum_fusion.28
  8.8 4.1 %collective-permute-start.4 = (f32[5,4,6,720]{3,2,1,0:T(8,128)}, f32[5,4,6,720]{3,2,1,0:T(8,128)}, u32[]{:S(2)}, u32[]{:S(2)}) collective-permute-start(f32[5,4,6,720]{3,2,1,0:T(8,128)} %pad_maximum_fusion.28), channel_id=1, source_target_pairs={{0,2},{1,3},{2,0},{3,1},{4,6},{5,7},{6,4},{7,5},{8,10},{9,11},{10,... | collective-permute-start | bytes 1036808 | tf_op jit(solution)/shard_map/ppermute | solution.py:29
  12.8 1.0 pad_maximum_fusion.25
  13.8 0.9 fusion.122
  14.8 2.6 %collective-permute-start.1 = (f32[28,3,720]{2,1,0:T(4,128)}, f32[28,3,720]{2,1,0:T(4,128)S(1)}, u32[]{:S(2)}, u32[]{:S(2)}) collective-permute-start(f32[28,3,720]{2,1,0:T(4,128)} %get-tuple-element.24), channel_id=1, source_target_pairs={{4,0},{8,4},{12,8},{16,12},{20,16},{24,20},{28,24},{0,28},{5,1},{9... | collective-permute-start | bytes 725768 | tf_op jit(solution)/shard_map/ppermute | solution.py:20
  17.6 10.8 %fusion.5 = (f32[720,720]{1,0:T(8,128)S(1)}, f32[720,720]{1,0:T(8,128)}) fusion(s32[720]{0:T(1024)S(1)} %iota_add_fusion), kind=kLoop, calls=%fused_computation.8 | loop fusion | flops 4665600 | bytes 4150080 | tf_op jit(solution)/shard_map/cos | solution.py:64
  28.4 1.4 fusion.12
  29.9 1.6 collective-permute-start.2
  31.5 2.2 collective-permute-start.3
  33.8 0.8 abs_multiply_fusion.1
  34.6 5.6 %collective-permute-done.2 = f32[28,14,3]{2,1,0:T(8,128)S(1)} collective-permute-done((f32[28,14,3]{2,1,0:T(8,128)S(1)}, f32[28,14,3]{2,1,0:T(8,128)S(1)}, u32[]{:S(2)}, u32[]{:S(2)}) %collective-permute-start.2) | collective-permute-done | bytes 4736 | tf_op jit(solution)/shard_map/ppermute | solution.py:18
  40.2 4.4 %collective-permute-done.3 = f32[28,14,3]{2,1,0:T(8,128)S(1)} collective-permute-done((f32[28,14,3]{2,1,0:T(8,128)S(1)}, f32[28,14,3]{2,1,0:T(8,128)S(1)}, u32[]{:S(2)}, u32[]{:S(2)}) %collective-permute-start.3) | collective-permute-done | bytes 4736 | tf_op jit(solution)/shard_map/ppermute | solution.py:20
  44.6 1.7 fusion.60
  46.8 0.9 broadcast_compare_fusion.3
  47.8 1.0 slice.329
  48.8 1.4 fusion.98
  50.2 2.1 fusion.125
  52.2 3.7 %rev.12 = f32[5,4,3,720]{3,2,1,0:T(4,128)} reverse(f32[5,4,3,720]{3,2,1,0:T(4,128)} %get-tuple-element.29), dimensions={2} | reverse | bytes 345600 | tf_op jit(solution)/shard_map/rev | solution.py:107
  56.0 3.7 %rev.13 = f32[5,4,3,720]{3,2,1,0:T(4,128)} reverse(f32[5,4,3,720]{3,2,1,0:T(4,128)} %get-tuple-element.30), dimensions={2} | reverse | bytes 345600 | tf_op jit(solution)/shard_map/rev | solution.py:111
  59.7 1.3 slice_select_fusion.3
  61.0 1.2 pad_maximum_fusion.21
  63.4 1.0 fusion.43
  64.8 1.4 copy-done
  66.2 4.2 %fusion.10 = f32[160,1440]{1,0:T(8,128)} fusion(f32[160,720]{1,0:T(8,128)S(1)} %bitcast.30, f32[720,720]{1,0:T(8,128)S(1)} %copy-done, f32[720,720]{1,0:T(8,128)S(1)} %get-tuple-element.41), kind=kOutput, calls=%fused_computation.13 | convolution fusion | flops 1991692800 | bytes 5529600 | tf_op jit(solution)/shard_map/dot_general | solution.py:128
  71.0 0.9 fusion.107
  71.8 49.4 %all-reduce.3.cloned.1.call-done = f32[160,1440]{1,0:T(8,128)} async-done(((f32[160,1440]{1,0:T(8,128)}), f32[160,1440]{1,0:T(8,128)}) %all-reduce.3.cloned.1.call-update) | async-done | bytes 921616 | tf_op jit(solution)/shard_map/psum | solution.py:129
  121.3 6.8 %fusion.15 = f32[160,720]{1,0:T(8,128)S(1)} fusion(f32[160,720]{1,0:T(8,128)S(1)} %bitcast.31, f32[720,720]{1,0:T(8,128)} %get-tuple-element.42, f32[720,720]{1,0:T(8,128)S(1)} %get-tuple-element.41, f32[160,1440]{1,0:T(8,128)} %all-reduce.3.cloned.1.call-done, f32[160,720]{1,0:T(8,128)} %fusion.107, pred[160]{0:T(512)(128)(4,1)S(1)} %broadcast_in_dim.83), kind=kOutput, calls=%fused_computation.34 | convolution fusion | flops 1992268800 | bytes 6451360 | tf_op jit(solution)/shard_map/dot_general | solution.py:131
  128.3 2.6 %collective-permute-start.6 = (f32[28,3,720]{2,1,0:T(4,128)S(1)}, f32[28,3,720]{2,1,0:T(4,128)S(1)}, u32[]{:S(2)}, u32[]{:S(2)}) collective-permute-start(f32[28,3,720]{2,1,0:T(4,128)S(1)} %get-tuple-element.22), channel_id=1, source_target_pairs={{4,0},{8,4},{12,8},{16,12},{20,16},{24,20},{28,24},{0,28},{5,1},{9... | collective-permute-start | bytes 725768 | tf_op jit(solution)/shard_map/ppermute | solution.py:20
  131.1 1.7 collective-permute-start.9
  132.8 5.0 %collective-permute-done.5 = f32[28,3,720]{2,1,0:T(4,128)S(1)} collective-permute-done((f32[28,3,720]{2,1,0:T(4,128)S(1)}, f32[28,3,720]{2,1,0:T(4,128)S(1)}, u32[]{:S(2)}, u32[]{:S(2)}) %collective-permute-start.5) | collective-permute-done | bytes 241952 | tf_op jit(solution)/shard_map/ppermute | solution.py:18
  138.2 1.3 collective-permute-start.7
  139.5 2.5 %collective-permute-start.8 = (f32[28,14,3]{2,1,0:T(8,128)S(1)}, f32[28,14,3]{2,1,0:T(8,128)S(1)}, u32[]{:S(2)}, u32[]{:S(2)}) collective-permute-start(f32[28,14,3]{2,1,0:T(8,128)S(1)} %get-tuple-element.14), channel_id=1, source_target_pairs={{1,0},{2,1},{3,2},{0,3},{5,4},{6,5},{7,6},{4,7},{9,8},{10,9},{11,1... | collective-permute-start | bytes 14120 | tf_op jit(solution)/shard_map/ppermute | solution.py:20
  142.1 0.8 abs_multiply_fusion
  142.9 7.7 %collective-permute-done.7 = f32[28,14,3]{2,1,0:T(8,128)S(1)} collective-permute-done((f32[28,14,3]{2,1,0:T(8,128)S(1)}, f32[28,14,3]{2,1,0:T(8,128)S(1)}, u32[]{:S(2)}, u32[]{:S(2)}) %collective-permute-start.7) | collective-permute-done | bytes 4736 | tf_op jit(solution)/shard_map/ppermute | solution.py:18
  150.7 11.3 %collective-permute-done.8 = f32[28,14,3]{2,1,0:T(8,128)S(1)} collective-permute-done((f32[28,14,3]{2,1,0:T(8,128)S(1)}, f32[28,14,3]{2,1,0:T(8,128)S(1)}, u32[]{:S(2)}, u32[]{:S(2)}) %collective-permute-start.8) | collective-permute-done | bytes 4736 | tf_op jit(solution)/shard_map/ppermute | solution.py:20
  162.0 0.7 fusion.64
  163.2 1.0 slice.362
  164.2 1.4 fusion.80
  165.6 0.9 fusion.123
  166.5 3.8 %rev.14 = f32[5,4,3,720]{3,2,1,0:T(4,128)} reverse(f32[5,4,3,720]{3,2,1,0:T(4,128)} %get-tuple-element.25), dimensions={2} | reverse | bytes 345600 | tf_op jit(solution)/shard_map/rev | solution.py:107
  170.2 3.8 %rev.15 = f32[5,4,3,720]{3,2,1,0:T(4,128)} reverse(f32[5,4,3,720]{3,2,1,0:T(4,128)} %get-tuple-element.26), dimensions={2} | reverse | bytes 345600 | tf_op jit(solution)/shard_map/rev | solution.py:111
  174.0 1.6 slice_select_fusion.1
  177.0 1.0 fusion.26
  178.2 1.4 copy-done.1
  179.6 4.2 %fusion.8 = f32[160,1440]{1,0:T(8,128)} fusion(f32[160,720]{1,0:T(8,128)S(1)} %bitcast.32, f32[720,720]{1,0:T(8,128)S(1)} %copy-done.1, f32[720,720]{1,0:T(8,128)S(1)} %get-tuple-element.41), kind=kOutput, calls=%fused_computation.11 | convolution fusion | flops 1991692800 | bytes 5529600 | tf_op jit(solution)/shard_map/dot_general | solution.py:128
  183.8 49.9 %all-reduce.5.cloned.1.call-done = f32[160,1440]{1,0:T(8,128)} async-done(((f32[160,1440]{1,0:T(8,128)}), f32[160,1440]{1,0:T(8,128)}) %all-reduce.5.cloned.1.call-update) | async-done | bytes 921616 | tf_op jit(solution)/shard_map/psum | solution.py:129
  233.7 7.3 %fusion.16 = f32[160,720]{1,0:T(8,128)} fusion(f32[160,720]{1,0:T(8,128)S(1)} %bitcast.33, f32[720,720]{1,0:T(8,128)} %get-tuple-element.42, f32[720,720]{1,0:T(8,128)S(1)} %get-tuple-element.41, f32[160,1440]{1,0:T(8,128)} %all-reduce.5.cloned.1.call-done, f32[160,720]{1,0:T(8,128)S(1)} %copy-done.14, pred[160]{0:T(512)(128)(4,1)S(1)} %broadcast_in_dim.83), kind=kOutput, calls=%fused_computation.35 | convolution fusion | flops 1992268800 | bytes 6451360 | tf_op jit(solution)/shard_map/dot_general | solution.py:131
  (86 shorter events, 5.8 us)
Async XLA Ops:
  6.5 6.3 %copy-start.3 = (f32[5,4,8,720]{3,2,1,0:T(8,128)S(1)}, f32[5,4,8,720]{3,2,1,0:T(8,128)}, u32[]{:S(2)}) copy-start(f32[5,4,8,720]{3,2,1,0:T(8,128)} %param.4) | copy-start | bytes 1382404
  6.5 114.7 %all-reduce.3.cloned.1.call-start = ((), (), s32[]{:S(2)}) async-start(), calls=%async_computation | async-start | bytes 1966080 | tf_op jit(solution)/shard_map/psum | solution.py:129
  8.8 41.4 %collective-permute-start.4 = (f32[5,4,6,720]{3,2,1,0:T(8,128)}, f32[5,4,6,720]{3,2,1,0:T(8,128)}, u32[]{:S(2)}, u32[]{:S(2)}) collective-permute-start(f32[5,4,6,720]{3,2,1,0:T(8,128)} %pad_maximum_fusion.28), channel_id=1, source_target_pairs={{0,2},{1,3},{2,0},{3,1},{4,6},{5,7},{6,4},{7,5},{8,10},{9,11},{10,... | collective-permute-start | bytes 1036808 | tf_op jit(solution)/shard_map/ppermute | solution.py:29
  14.8 13.5 %collective-permute-start = (f32[28,3,720]{2,1,0:T(4,128)}, f32[28,3,720]{2,1,0:T(4,128)}, u32[]{:S(2)}, u32[]{:S(2)}) collective-permute-start(f32[28,3,720]{2,1,0:T(4,128)} %get-tuple-element.23), channel_id=1, source_target_pairs={{0,4},{4,8},{8,12},{12,16},{16,20},{20,24},{24,28},{28,0},{1,5},{5... | collective-permute-start | bytes 725768 | tf_op jit(solution)/shard_map/ppermute | solution.py:18
  14.8 13.5 %collective-permute-start.1 = (f32[28,3,720]{2,1,0:T(4,128)}, f32[28,3,720]{2,1,0:T(4,128)S(1)}, u32[]{:S(2)}, u32[]{:S(2)}) collective-permute-start(f32[28,3,720]{2,1,0:T(4,128)} %get-tuple-element.24), channel_id=1, source_target_pairs={{4,0},{8,4},{12,8},{16,12},{20,16},{24,20},{28,24},{0,28},{5,1},{9... | collective-permute-start | bytes 725768 | tf_op jit(solution)/shard_map/ppermute | solution.py:20
  17.5 10.8 %copy-start.6 = (f32[4,8,720]{2,1,0:T(8,128)S(1)}, f32[4,8,720]{2,1,0:T(8,128)}, u32[]{:S(2)}) copy-start(f32[4,8,720]{2,1,0:T(8,128)} %param.6) | copy-start | bytes 276484
  17.6 10.8 %copy-start.7 = (f32[4,8,720]{2,1,0:T(8,128)S(1)}, f32[4,8,720]{2,1,0:T(8,128)}, u32[]{:S(2)}) copy-start(f32[4,8,720]{2,1,0:T(8,128)} %param.5) | copy-start | bytes 276484
  28.3 16.3 %copy-start.4 = (f32[5,4,8,720]{3,2,1,0:T(8,128)S(1)}, f32[5,4,8,720]{3,2,1,0:T(8,128)}, u32[]{:S(2)}) copy-start(f32[5,4,8,720]{3,2,1,0:T(8,128)} %param.4) | copy-start | bytes 1382404
  28.4 5.4 %copy-start.10 = (f32[28,3,720]{2,1,0:T(4,128)}, f32[28,3,720]{2,1,0:T(4,128)S(1)}, u32[]{:S(2)}) copy-start(f32[28,3,720]{2,1,0:T(4,128)S(1)} %collective-permute-done.1) | copy-start | bytes 725764
  29.9 10.4 %collective-permute-start.2 = (f32[28,14,3]{2,1,0:T(8,128)S(1)}, f32[28,14,3]{2,1,0:T(8,128)S(1)}, u32[]{:S(2)}, u32[]{:S(2)}) collective-permute-start(f32[28,14,3]{2,1,0:T(8,128)S(1)} %get-tuple-element.15), channel_id=1, source_target_pairs={{0,1},{1,2},{2,3},{3,0},{4,5},{5,6},{6,7},{7,4},{8,9},{9,10},{10,1... | collective-permute-start | bytes 14120 | tf_op jit(solution)/shard_map/ppermute | solution.py:18
  31.5 13.1 %collective-permute-start.3 = (f32[28,14,3]{2,1,0:T(8,128)S(1)}, f32[28,14,3]{2,1,0:T(8,128)S(1)}, u32[]{:S(2)}, u32[]{:S(2)}) collective-permute-start(f32[28,14,3]{2,1,0:T(8,128)S(1)} %get-tuple-element.16), channel_id=1, source_target_pairs={{1,0},{2,1},{3,2},{0,3},{5,4},{6,5},{7,6},{4,7},{9,8},{10,9},{11,1... | collective-permute-start | bytes 14120 | tf_op jit(solution)/shard_map/ppermute | solution.py:20
  33.8 6.4 %copy-start.17 = (f32[4,9,720]{2,1,0:T(8,128)}, f32[4,9,720]{2,1,0:T(8,128)S(1)}, u32[]{:S(2)}) copy-start(f32[4,9,720]{2,1,0:T(8,128)S(1)} %get-tuple-element.12) | copy-start | bytes 311044
  34.6 12.2 %copy-start.11 = (f32[28,3,720]{2,1,0:T(4,128)S(1)}, f32[28,3,720]{2,1,0:T(4,128)}, u32[]{:S(2)}) copy-start(f32[28,3,720]{2,1,0:T(4,128)} %copy-done.10) | copy-start | bytes 725764
  59.7 2.6 %copy-start.9 = (f32[5,4,8,720]{3,2,1,0:T(8,128)S(1)}, f32[5,4,8,720]{3,2,1,0:T(8,128)}, u32[]{:S(2)}) copy-start(f32[5,4,8,720]{3,2,1,0:T(8,128)} %slice.329) | copy-start | bytes 1382404
  62.2 0.9 copy-start.18
  62.3 1.0 copy-start.21
  62.3 1.1 copy-start.22
  63.4 1.0 copy-start.5
  63.4 1.2 copy-start.13
  64.5 1.6 copy-start
  66.2 4.6 %copy-start.23 = (s32[64]{0:T(128)S(1)}, s32[64]{0:T(128)}, u32[]{:S(2)}) copy-start(s32[64]{0:T(128)} %param.7) | copy-start | bytes 772
  70.4 163.3 %all-reduce.5.cloned.1.call-start = ((), (), s32[]{:S(2)}) async-start(), calls=%async_computation.1 | async-start | bytes 1966080 | tf_op jit(solution)/shard_map/psum | solution.py:129
  128.3 9.5 %collective-permute-start.5 = (f32[28,3,720]{2,1,0:T(4,128)S(1)}, f32[28,3,720]{2,1,0:T(4,128)S(1)}, u32[]{:S(2)}, u32[]{:S(2)}) collective-permute-start(f32[28,3,720]{2,1,0:T(4,128)S(1)} %get-tuple-element.21), channel_id=1, source_target_pairs={{0,4},{4,8},{8,12},{12,16},{16,20},{20,24},{24,28},{28,0},{1,5},{5... | collective-permute-start | bytes 725768 | tf_op jit(solution)/shard_map/ppermute | solution.py:18
  128.3 9.5 %collective-permute-start.6 = (f32[28,3,720]{2,1,0:T(4,128)S(1)}, f32[28,3,720]{2,1,0:T(4,128)S(1)}, u32[]{:S(2)}, u32[]{:S(2)}) collective-permute-start(f32[28,3,720]{2,1,0:T(4,128)S(1)} %get-tuple-element.22), channel_id=1, source_target_pairs={{4,0},{8,4},{12,8},{16,12},{20,16},{24,20},{28,24},{0,28},{5,1},{9... | collective-permute-start | bytes 725768 | tf_op jit(solution)/shard_map/ppermute | solution.py:20
  131.1 34.5 %collective-permute-start.9 = (f32[5,4,6,720]{3,2,1,0:T(8,128)S(1)}, f32[5,4,6,720]{3,2,1,0:T(8,128)S(1)}, u32[]{:S(2)}, u32[]{:S(2)}) collective-permute-start(f32[5,4,6,720]{3,2,1,0:T(8,128)S(1)} %pad_maximum_fusion.29), channel_id=1, source_target_pairs={{0,2},{1,3},{2,0},{3,1},{4,6},{5,7},{6,4},{7,5},{8,10},{9,11},{10,... | collective-permute-start | bytes 1036808 | tf_op jit(solution)/shard_map/ppermute | solution.py:29
  138.2 12.5 %collective-permute-start.7 = (f32[28,14,3]{2,1,0:T(8,128)S(1)}, f32[28,14,3]{2,1,0:T(8,128)S(1)}, u32[]{:S(2)}, u32[]{:S(2)}) collective-permute-start(f32[28,14,3]{2,1,0:T(8,128)S(1)} %get-tuple-element.13), channel_id=1, source_target_pairs={{0,1},{1,2},{2,3},{3,0},{4,5},{5,6},{6,7},{7,4},{8,9},{9,10},{10,1... | collective-permute-start | bytes 14120 | tf_op jit(solution)/shard_map/ppermute | solution.py:18
  139.5 22.4 %collective-permute-start.8 = (f32[28,14,3]{2,1,0:T(8,128)S(1)}, f32[28,14,3]{2,1,0:T(8,128)S(1)}, u32[]{:S(2)}, u32[]{:S(2)}) collective-permute-start(f32[28,14,3]{2,1,0:T(8,128)S(1)} %get-tuple-element.14), channel_id=1, source_target_pairs={{1,0},{2,1},{3,2},{0,3},{5,4},{6,5},{7,6},{4,7},{9,8},{10,9},{11,1... | collective-permute-start | bytes 14120 | tf_op jit(solution)/shard_map/ppermute | solution.py:20
  142.1 8.6 %copy-start.15 = (f32[4,9,720]{2,1,0:T(8,128)}, f32[4,9,720]{2,1,0:T(8,128)S(1)}, u32[]{:S(2)}) copy-start(f32[4,9,720]{2,1,0:T(8,128)S(1)} %get-tuple-element.8) | copy-start | bytes 311044
  162.6 1.6 copy-start.2
  165.6 10.0 %copy-start.8 = (f32[5,4,8,720]{3,2,1,0:T(8,128)S(1)}, f32[5,4,8,720]{3,2,1,0:T(8,128)}, u32[]{:S(2)}) copy-start(f32[5,4,8,720]{3,2,1,0:T(8,128)} %slice.362) | copy-start | bytes 1382404
  175.8 0.9 copy-start.16
  175.8 1.0 copy-start.19
  175.9 1.1 copy-start.20
  177.0 1.0 copy-start.12
  178.0 1.6 copy-start.1
  179.6 54.1 %copy-start.14 = (f32[160,720]{1,0:T(8,128)S(1)}, f32[160,720]{1,0:T(8,128)}, u32[]{:S(2)}) copy-start(f32[160,720]{1,0:T(8,128)} %fusion.107) | copy-start | bytes 1382404
Sparse Core Ops, SparseCore 0:
  70.5 50.6 all-reduce.2
  184.0 49.7 all-reduce.4
where the time goes:
time: 250 us; the launch traced here: 248 us
  waiting for transfers between devices  133 us (53%)
  other arithmetic  31.8 us (13%)
  local copies, waits for them, and re-layouts  27.3 us (11%)
  matrix products  22.5 us (9%)
  starting transfers between devices  19 us (8%)
  between operations  13.8 us (6%)
    psum x2, waiting for transfers between devices, on_device(): spectra = lax.psum(partial_value, 'lon')  99.3 us
    ppermute x4, waiting for transfers between devices, extended_2(): lax.ppermute(tail, axis, [(i, (i + 1) % count) for i in range(count)])  18.3 us
    ppermute x4, waiting for transfers between devices, extended_2(): lax.ppermute(head, axis, [((i + 1) % count, i) for i in range(count)])  15.7 us
    dot_general x2, matrix products, on_device(): smooth = jnp.dot(weighted, basis_tile.T, precision=lax.Precision.HIGHEST)  14.1 us
    cos x1, other arithmetic, dft_basis(): return jnp.concatenate([jnp.cos(phase_angle), jnp.sin(phase_angle)], axis=1)  10.8 us
    ppermute x4, starting transfers between devices, extended_2(): lax.ppermute(head, axis, [((i + 1) % count, i) for i in range(count)])  10.1 us
    dot_general x2, matrix products, on_device(): jnp.dot(flat_rows, basis_tile, precision=lax.Precision.HIGHEST)  8.42 us
    rev x2, local copies, waits for them, and re-layouts, on_device(): antipodal[:, :, 2::-1]  7.49 us
  transfers between devices with their start and end apart: 12, of which 7 were waited for; matrix products, arithmetic and copies ran while one was open for 11% of the time, Pallas kernels for 0%

commit v1 on v0

--- a/solution.py
+++ b/solution.py
@@ -126,7 +126,9 @@
         band_cuts = lax.dynamic_slice_in_dim(cutoffs, lat_index * lat_rows, lat_rows)
         cut_rows = jnp.tile(band_cuts, field_count)
         partial_value = jnp.dot(flat_rows, basis_tile, precision=lax.Precision.HIGHEST)
-        spectra = lax.psum(partial_value, "lon")
+        spectra = partial_value
+        for hop in (1, 2):
+            spectra = spectra + lax.ppermute(spectra, "lon", [(dev, dev ^ hop) for dev in range(4)])
         weighted = spectra * mode_weights(cut_rows, circle)
         smooth = jnp.dot(weighted, basis_tile.T, precision=lax.Precision.HIGHEST)
         polar_flat = jnp.tile(polar_rows, field_count)

time: 250 us -> 271 us (1.084)
  waiting for transfers between devices: 133 us -> 161 us
  between operations: 13.8 us -> 0.46 us
  starting transfers between devices: 19 us -> 28.4 us
  matrix products: 22.5 us -> 18.7 us
    ppermute x0 -> x4, waiting for transfers between devices: none -> 126 us  [on_device(): lax.ppermute(spectra, 'lon', [(dev, dev ^ hop) for dev in range(4)])]
    psum x2 -> x0, waiting for transfers between devices: 99.3 us -> none  [on_device(): spectra = lax.psum(partial_value, 'lon')]
    ppermute x0 -> x4, starting transfers between devices: none -> 8.93 us  [on_device(): lax.ppermute(spectra, 'lon', [(dev, dev ^ hop) for dev in range(4)])]
  transfers between devices with their start and end apart: 12 -> 14, of which waited for: 7 -> 10; matrix products, arithmetic and copies ran while one was open for 11% -> 10% of each run, Pallas kernels for 0% -> 0%
where the time goes in v1:
time: 271 us; the launch traced here: 268 us
  waiting for transfers between devices  161 us (59%)
  other arithmetic  32.2 us (12%)
  starting transfers between devices  28.4 us (10%)
  local copies, waits for them, and re-layouts  27.3 us (10%)
  matrix products  18.7 us (7%)
    ppermute x4, waiting for transfers between devices, on_device(): lax.ppermute(spectra, 'lon', [(dev, dev ^ hop) for dev in range(4)])  126 us
    ppermute x4, waiting for transfers between devices, extended_2(): lax.ppermute(tail, axis, [(i, (i + 1) % count) for i in range(count)])  18.3 us
    ppermute x4, waiting for transfers between devices, extended_2(): lax.ppermute(head, axis, [((i + 1) % count, i) for i in range(count)])  16.4 us
    ppermute x4, starting transfers between devices, extended_2(): lax.ppermute(head, axis, [((i + 1) % count, i) for i in range(count)])  12.2 us
    dot_general x2, matrix products, on_device(): smooth = jnp.dot(weighted, basis_tile.T, precision=lax.Precision.HIGHEST)  12.2 us
    cos x1, other arithmetic, dft_basis(): return jnp.concatenate([jnp.cos(phase_angle), jnp.sin(phase_angle)], axis=1)  10.8 us
    ppermute x4, starting transfers between devices, on_device(): lax.ppermute(spectra, 'lon', [(dev, dev ^ hop) for dev in range(4)])  8.93 us
    rev x2, local copies, waits for them, and re-layouts, on_device(): antipodal[:, :, 5:2:-1]  7.47 us
  transfers between devices with their start and end apart: 14, of which 10 were waited for; matrix products, arithmetic and copies ran while one was open for 10% of the time, Pallas kernels for 0%

profile of v1, /device:TPU:0, one launch (start us, length us, event | category | flops | bytes accessed | tf_op | source)
XLA Modules:
  0.0 267.6 jit_solution(14268148471364191440)
XLA Ops:
  0.0 1.3 fusion.128
  2.2 4.1 %collective-permute-start.4 = (f32[5,4,6,720]{3,2,1,0:T(8,128)}, f32[5,4,6,720]{3,2,1,0:T(8,128)}, u32[]{:S(2)}, u32[]{:S(2)}) collective-permute-start(f32[5,4,6,720]{3,2,1,0:T(8,128)} %pad_maximum_fusion.28), channel_id=1, source_target_pairs={{0,2},{1,3},{2,0},{3,1},{4,6},{5,7},{6,4},{7,5},{8,10},{9,11},{10,... | collective-permute-start | bytes 1036808 | tf_op jit(solution)/shard_map/ppermute | solution.py:29
  6.3 1.0 pad_maximum_fusion.25
  7.3 0.9 fusion.124
  8.2 2.6 collective-permute-start.1
  11.0 10.8 %fusion.5 = (f32[720,720]{1,0:T(8,128)S(1)}, f32[720,720]{1,0:T(8,128)}) fusion(s32[720]{0:T(1024)S(1)} %iota_add_fusion), kind=kLoop, calls=%fused_computation.8 | loop fusion | flops 4665600 | bytes 4150080 | tf_op jit(solution)/shard_map/cos | solution.py:64
  21.8 1.4 fusion.12
  23.3 1.6 collective-permute-start.2
  25.0 2.2 collective-permute-start.3
  28.1 5.6 %collective-permute-done.2 = f32[28,14,3]{2,1,0:T(8,128)S(1)} collective-permute-done((f32[28,14,3]{2,1,0:T(8,128)S(1)}, f32[28,14,3]{2,1,0:T(8,128)S(1)}, u32[]{:S(2)}, u32[]{:S(2)}) %collective-permute-start.2) | collective-permute-done | bytes 4736 | tf_op jit(solution)/shard_map/ppermute | solution.py:18
  33.7 4.4 %collective-permute-done.3 = f32[28,14,3]{2,1,0:T(8,128)S(1)} collective-permute-done((f32[28,14,3]{2,1,0:T(8,128)S(1)}, f32[28,14,3]{2,1,0:T(8,128)S(1)}, u32[]{:S(2)}, u32[]{:S(2)}) %collective-permute-start.3) | collective-permute-done | bytes 4736 | tf_op jit(solution)/shard_map/ppermute | solution.py:20
  38.1 1.7 fusion.60
  40.3 0.9 broadcast_compare_fusion.3
  41.2 1.0 slice.329
  42.2 1.4 fusion.100
  43.6 2.1 fusion.127
  45.6 3.7 %rev.12 = f32[5,4,3,720]{3,2,1,0:T(4,128)} reverse(f32[5,4,3,720]{3,2,1,0:T(4,128)} %get-tuple-element.29), dimensions={2} | reverse | bytes 345600 | tf_op jit(solution)/shard_map/rev | solution.py:107
  49.4 3.7 %rev.13 = f32[5,4,3,720]{3,2,1,0:T(4,128)} reverse(f32[5,4,3,720]{3,2,1,0:T(4,128)} %get-tuple-element.30), dimensions={2} | reverse | bytes 345600 | tf_op jit(solution)/shard_map/rev | solution.py:111
  53.1 1.3 slice_select_fusion.3
  54.5 1.2 pad_maximum_fusion.21
  56.8 1.0 fusion.43
  58.2 1.4 copy-done
  59.6 3.3 %fusion.10 = f32[160,1440]{1,0:T(8,128)S(1)} fusion(f32[160,720]{1,0:T(8,128)S(1)} %bitcast.30, f32[720,720]{1,0:T(8,128)S(1)} %copy-done, f32[720,720]{1,0:T(8,128)S(1)} %get-tuple-element.41), kind=kOutput, calls=%fused_computation.13 | convolution fusion | flops 1991692800 | bytes 5529600 | tf_op jit(solution)/shard_map/dot_general | solution.py:128
  63.7 21.9 %collective-permute-done.5 = f32[160,1440]{1,0:T(8,128)S(1)} collective-permute-done((f32[160,1440]{1,0:T(8,128)S(1)}, f32[160,1440]{1,0:T(8,128)S(1)}, u32[]{:S(2)}, u32[]{:S(2)}) %collective-permute-start.5) | collective-permute-done | bytes 921632 | tf_op jit(solution)/shard_map/ppermute | solution.py:131
  85.6 1.1 add.172
  86.7 2.7 %collective-permute-start.6 = (f32[160,1440]{1,0:T(8,128)}, f32[160,1440]{1,0:T(8,128)}, u32[]{:S(2)}, u32[]{:S(2)}) collective-permute-start(f32[160,1440]{1,0:T(8,128)} %add.172), channel_id=1, source_target_pairs={{0,2},{1,3},{2,0},{3,1},{4,6},{5,7},{6,4},{7,5},{8,10},{9,11},{10,... | collective-permute-start | bytes 2764808 | tf_op jit(solution)/shard_map/ppermute | solution.py:131
  89.9 41.0 %collective-permute-done.6 = f32[160,1440]{1,0:T(8,128)} collective-permute-done((f32[160,1440]{1,0:T(8,128)}, f32[160,1440]{1,0:T(8,128)}, u32[]{:S(2)}, u32[]{:S(2)}) %collective-permute-start.6) | collective-permute-done | bytes 921632 | tf_op jit(solution)/shard_map/ppermute | solution.py:131
  130.9 6.8 %fusion.15 = f32[160,720]{1,0:T(8,128)S(1)} fusion(f32[160,720]{1,0:T(8,128)S(1)} %bitcast.31, f32[720,720]{1,0:T(8,128)} %get-tuple-element.42, f32[720,720]{1,0:T(8,128)S(1)} %get-tuple-element.41, f32[160,720]{1,0:T(8,128)S(1)} %fusion.109, f32[160,1440]{1,0:T(8,128)} %add.172, f32[160,1440]{1,0:T(8,128)} %collective-permute-done.6, ...), kind=kOutput, calls=%fused_computation.34 | convolution fusion | flops 1992499200 | bytes 7372960 | tf_op jit(solution)/shard_map/dot_general | solution.py:133
  138.0 4.2 %collective-permute-start.8 = (f32[28,3,720]{2,1,0:T(4,128)S(1)}, f32[28,3,720]{2,1,0:T(4,128)S(1)}, u32[]{:S(2)}, u32[]{:S(2)}) collective-permute-start(f32[28,3,720]{2,1,0:T(4,128)S(1)} %get-tuple-element.22), channel_id=1, source_target_pairs={{4,0},{8,4},{12,8},{16,12},{20,16},{24,20},{28,24},{0,28},{5,1},{9... | collective-permute-start | bytes 725768 | tf_op jit(solution)/shard_map/ppermute | solution.py:20
  142.5 5.1 %collective-permute-done.7 = f32[28,3,720]{2,1,0:T(4,128)S(1)} collective-permute-done((f32[28,3,720]{2,1,0:T(4,128)S(1)}, f32[28,3,720]{2,1,0:T(4,128)S(1)}, u32[]{:S(2)}, u32[]{:S(2)}) %collective-permute-start.7) | collective-permute-done | bytes 241952 | tf_op jit(solution)/shard_map/ppermute | solution.py:18
  148.7 1.4 collective-permute-start.9
  150.1 3.1 %collective-permute-start.10 = (f32[28,14,3]{2,1,0:T(8,128)S(1)}, f32[28,14,3]{2,1,0:T(8,128)S(1)}, u32[]{:S(2)}, u32[]{:S(2)}) collective-permute-start(f32[28,14,3]{2,1,0:T(8,128)S(1)} %get-tuple-element.14), channel_id=1, source_target_pairs={{1,0},{2,1},{3,2},{0,3},{5,4},{6,5},{7,6},{4,7},{9,8},{10,9},{11,1... | collective-permute-start | bytes 14120 | tf_op jit(solution)/shard_map/ppermute | solution.py:20
  154.1 7.5 %collective-permute-done.9 = f32[28,14,3]{2,1,0:T(8,128)S(1)} collective-permute-done((f32[28,14,3]{2,1,0:T(8,128)S(1)}, f32[28,14,3]{2,1,0:T(8,128)S(1)}, u32[]{:S(2)}, u32[]{:S(2)}) %collective-permute-start.9) | collective-permute-done | bytes 4736 | tf_op jit(solution)/shard_map/ppermute | solution.py:18
  161.6 11.3 %collective-permute-done.10 = f32[28,14,3]{2,1,0:T(8,128)S(1)} collective-permute-done((f32[28,14,3]{2,1,0:T(8,128)S(1)}, f32[28,14,3]{2,1,0:T(8,128)S(1)}, u32[]{:S(2)}, u32[]{:S(2)}) %collective-permute-start.10) | collective-permute-done | bytes 4736 | tf_op jit(solution)/shard_map/ppermute | solution.py:20
  174.2 1.0 slice.362
  175.2 1.4 fusion.82
  176.5 0.9 fusion.125
  177.4 3.7 %rev.14 = f32[5,4,3,720]{3,2,1,0:T(4,128)} reverse(f32[5,4,3,720]{3,2,1,0:T(4,128)} %get-tuple-element.25), dimensions={2} | reverse | bytes 345600 | tf_op jit(solution)/shard_map/rev | solution.py:107
  181.2 3.7 %rev.15 = f32[5,4,3,720]{3,2,1,0:T(4,128)} reverse(f32[5,4,3,720]{3,2,1,0:T(4,128)} %get-tuple-element.26), dimensions={2} | reverse | bytes 345600 | tf_op jit(solution)/shard_map/rev | solution.py:111
  184.9 1.6 slice_select_fusion.1
  187.8 1.0 fusion.26
  189.1 1.4 copy-done.1
  190.5 3.2 %fusion.8 = f32[160,1440]{1,0:T(8,128)S(1)} fusion(f32[160,720]{1,0:T(8,128)S(1)} %bitcast.32, f32[720,720]{1,0:T(8,128)S(1)} %copy-done.1, f32[720,720]{1,0:T(8,128)S(1)} %get-tuple-element.41), kind=kOutput, calls=%fused_computation.11 | convolution fusion | flops 1991692800 | bytes 5529600 | tf_op jit(solution)/shard_map/dot_general | solution.py:128
  193.7 3.0 %collective-permute-start.12 = (f32[160,1440]{1,0:T(8,128)S(1)}, f32[160,1440]{1,0:T(8,128)S(1)}, u32[]{:S(2)}, u32[]{:S(2)}) collective-permute-start(f32[160,1440]{1,0:T(8,128)S(1)} %fusion.8), channel_id=1, source_target_pairs={{0,1},{1,0},{2,3},{3,2},{4,5},{5,4},{6,7},{7,6},{8,9},{9,8},{10,11... | collective-permute-start | bytes 2764808 | tf_op jit(solution)/shard_map/ppermute | solution.py:131
  196.7 20.9 %collective-permute-done.12 = f32[160,1440]{1,0:T(8,128)S(1)} collective-permute-done((f32[160,1440]{1,0:T(8,128)S(1)}, f32[160,1440]{1,0:T(8,128)S(1)}, u32[]{:S(2)}, u32[]{:S(2)}) %collective-permute-start.12) | collective-permute-done | bytes 921632 | tf_op jit(solution)/shard_map/ppermute | solution.py:131
  217.8 2.4 collective-permute-start.13
  220.2 42.0 %collective-permute-done.13 = f32[160,1440]{1,0:T(8,128)S(1)} collective-permute-done((f32[160,1440]{1,0:T(8,128)S(1)}, f32[160,1440]{1,0:T(8,128)S(1)}, u32[]{:S(2)}, u32[]{:S(2)}) %collective-permute-start.13) | collective-permute-done | bytes 921632 | tf_op jit(solution)/shard_map/ppermute | solution.py:131
  262.2 5.4 %fusion.16 = f32[160,720]{1,0:T(8,128)} fusion(f32[160,720]{1,0:T(8,128)S(1)} %bitcast.33, f32[720,720]{1,0:T(8,128)S(1)} %copy-done.1, f32[720,720]{1,0:T(8,128)S(1)} %get-tuple-element.41, f32[160,720]{1,0:T(8,128)S(1)} %copy-done.15, f32[160,1440]{1,0:T(8,128)S(1)} %add.188, f32[160,1440]{1,0:T(8,128)S(1)} %collective-permute-done.13, ...), kind=kOutput, calls=%fused_computation.35 | convolution fusion | flops 1992499200 | bytes 7372960 | tf_op jit(solution)/shard_map/dot_general | solution.py:133
  (92 shorter events, 10.6 us)
Async XLA Ops:
  0.0 6.3 %copy-start.3 = (f32[5,4,8,720]{3,2,1,0:T(8,128)S(1)}, f32[5,4,8,720]{3,2,1,0:T(8,128)}, u32[]{:S(2)}) copy-start(f32[5,4,8,720]{3,2,1,0:T(8,128)} %param.4) | copy-start | bytes 1382404
  2.2 41.4 %collective-permute-start.4 = (f32[5,4,6,720]{3,2,1,0:T(8,128)}, f32[5,4,6,720]{3,2,1,0:T(8,128)}, u32[]{:S(2)}, u32[]{:S(2)}) collective-permute-start(f32[5,4,6,720]{3,2,1,0:T(8,128)} %pad_maximum_fusion.28), channel_id=1, source_target_pairs={{0,2},{1,3},{2,0},{3,1},{4,6},{5,7},{6,4},{7,5},{8,10},{9,11},{10,... | collective-permute-start | bytes 1036808 | tf_op jit(solution)/shard_map/ppermute | solution.py:29
  8.2 13.6 %collective-permute-start = (f32[28,3,720]{2,1,0:T(4,128)}, f32[28,3,720]{2,1,0:T(4,128)}, u32[]{:S(2)}, u32[]{:S(2)}) collective-permute-start(f32[28,3,720]{2,1,0:T(4,128)} %get-tuple-element.23), channel_id=1, source_target_pairs={{0,4},{4,8},{8,12},{12,16},{16,20},{20,24},{24,28},{28,0},{1,5},{5... | collective-permute-start | bytes 725768 | tf_op jit(solution)/shard_map/ppermute | solution.py:18
  8.2 13.6 %collective-permute-start.1 = (f32[28,3,720]{2,1,0:T(4,128)}, f32[28,3,720]{2,1,0:T(4,128)S(1)}, u32[]{:S(2)}, u32[]{:S(2)}) collective-permute-start(f32[28,3,720]{2,1,0:T(4,128)} %get-tuple-element.24), channel_id=1, source_target_pairs={{4,0},{8,4},{12,8},{16,12},{20,16},{24,20},{28,24},{0,28},{5,1},{9... | collective-permute-start | bytes 725768 | tf_op jit(solution)/shard_map/ppermute | solution.py:20
  11.0 10.8 %copy-start.6 = (f32[4,8,720]{2,1,0:T(8,128)S(1)}, f32[4,8,720]{2,1,0:T(8,128)}, u32[]{:S(2)}) copy-start(f32[4,8,720]{2,1,0:T(8,128)} %param.6) | copy-start | bytes 276484
  11.0 10.8 %copy-start.7 = (f32[4,8,720]{2,1,0:T(8,128)S(1)}, f32[4,8,720]{2,1,0:T(8,128)}, u32[]{:S(2)}) copy-start(f32[4,8,720]{2,1,0:T(8,128)} %param.5) | copy-start | bytes 276484
  21.8 16.3 %copy-start.4 = (f32[5,4,8,720]{3,2,1,0:T(8,128)S(1)}, f32[5,4,8,720]{3,2,1,0:T(8,128)}, u32[]{:S(2)}) copy-start(f32[5,4,8,720]{3,2,1,0:T(8,128)} %param.4) | copy-start | bytes 1382404
  21.8 5.4 %copy-start.10 = (f32[28,3,720]{2,1,0:T(4,128)}, f32[28,3,720]{2,1,0:T(4,128)S(1)}, u32[]{:S(2)}) copy-start(f32[28,3,720]{2,1,0:T(4,128)S(1)} %collective-permute-done.1) | copy-start | bytes 725764
  23.3 10.4 %collective-permute-start.2 = (f32[28,14,3]{2,1,0:T(8,128)S(1)}, f32[28,14,3]{2,1,0:T(8,128)S(1)}, u32[]{:S(2)}, u32[]{:S(2)}) collective-permute-start(f32[28,14,3]{2,1,0:T(8,128)S(1)} %get-tuple-element.15), channel_id=1, source_target_pairs={{0,1},{1,2},{2,3},{3,0},{4,5},{5,6},{6,7},{7,4},{8,9},{9,10},{10,1... | collective-permute-start | bytes 14120 | tf_op jit(solution)/shard_map/ppermute | solution.py:18
  25.0 13.1 %collective-permute-start.3 = (f32[28,14,3]{2,1,0:T(8,128)S(1)}, f32[28,14,3]{2,1,0:T(8,128)S(1)}, u32[]{:S(2)}, u32[]{:S(2)}) collective-permute-start(f32[28,14,3]{2,1,0:T(8,128)S(1)} %get-tuple-element.16), channel_id=1, source_target_pairs={{1,0},{2,1},{3,2},{0,3},{5,4},{6,5},{7,6},{4,7},{9,8},{10,9},{11,1... | collective-permute-start | bytes 14120 | tf_op jit(solution)/shard_map/ppermute | solution.py:20
  27.3 6.4 %copy-start.18 = (f32[4,9,720]{2,1,0:T(8,128)}, f32[4,9,720]{2,1,0:T(8,128)S(1)}, u32[]{:S(2)}) copy-start(f32[4,9,720]{2,1,0:T(8,128)S(1)} %get-tuple-element.12) | copy-start | bytes 311044
  28.1 12.2 %copy-start.11 = (f32[28,3,720]{2,1,0:T(4,128)S(1)}, f32[28,3,720]{2,1,0:T(4,128)}, u32[]{:S(2)}) copy-start(f32[28,3,720]{2,1,0:T(4,128)} %copy-done.10) | copy-start | bytes 725764
  53.1 2.6 copy-start.9
  55.7 0.9 copy-start.19
  55.7 1.0 copy-start.22
  55.7 1.1 copy-start.23
  56.8 1.0 copy-start.5
  56.8 1.2 copy-start.13
  58.0 1.6 copy-start
  62.9 26.7 %copy-start.24 = (s32[64]{0:T(128)S(1)}, s32[64]{0:T(128)}, u32[]{:S(2)}) copy-start(s32[64]{0:T(128)} %param.7) | copy-start | bytes 772
  62.9 22.7 %collective-permute-start.5 = (f32[160,1440]{1,0:T(8,128)S(1)}, f32[160,1440]{1,0:T(8,128)S(1)}, u32[]{:S(2)}, u32[]{:S(2)}) collective-permute-start(f32[160,1440]{1,0:T(8,128)S(1)} %fusion.10), channel_id=1, source_target_pairs={{0,1},{1,0},{2,3},{3,2},{4,5},{5,4},{6,7},{7,6},{8,9},{9,8},{10,11... | collective-permute-start | bytes 2764808 | tf_op jit(solution)/shard_map/ppermute | solution.py:131
  86.7 44.2 %collective-permute-start.6 = (f32[160,1440]{1,0:T(8,128)}, f32[160,1440]{1,0:T(8,128)}, u32[]{:S(2)}, u32[]{:S(2)}) collective-permute-start(f32[160,1440]{1,0:T(8,128)} %add.172), channel_id=1, source_target_pairs={{0,2},{1,3},{2,0},{3,1},{4,6},{5,7},{6,4},{7,5},{8,10},{9,11},{10,... | collective-permute-start | bytes 2764808 | tf_op jit(solution)/shard_map/ppermute | solution.py:131
  89.9 47.9 %copy-start.14 = (f32[160,720]{1,0:T(8,128)}, f32[160,720]{1,0:T(8,128)S(1)}, u32[]{:S(2)}) copy-start(f32[160,720]{1,0:T(8,128)S(1)} %fusion.109) | copy-start | bytes 1382404
  137.9 9.7 %collective-permute-start.7 = (f32[28,3,720]{2,1,0:T(4,128)S(1)}, f32[28,3,720]{2,1,0:T(4,128)S(1)}, u32[]{:S(2)}, u32[]{:S(2)}) collective-permute-start(f32[28,3,720]{2,1,0:T(4,128)S(1)} %get-tuple-element.21), channel_id=1, source_target_pairs={{0,4},{4,8},{8,12},{12,16},{16,20},{20,24},{24,28},{28,0},{1,5},{5... | collective-permute-start | bytes 725768 | tf_op jit(solution)/shard_map/ppermute | solution.py:18
  138.0 10.3 %collective-permute-start.8 = (f32[28,3,720]{2,1,0:T(4,128)S(1)}, f32[28,3,720]{2,1,0:T(4,128)S(1)}, u32[]{:S(2)}, u32[]{:S(2)}) collective-permute-start(f32[28,3,720]{2,1,0:T(4,128)S(1)} %get-tuple-element.22), channel_id=1, source_target_pairs={{4,0},{8,4},{12,8},{16,12},{20,16},{24,20},{28,24},{0,28},{5,1},{9... | collective-permute-start | bytes 725768 | tf_op jit(solution)/shard_map/ppermute | solution.py:20
  142.4 34.1 %collective-permute-start.11 = (f32[5,4,6,720]{3,2,1,0:T(8,128)S(1)}, f32[5,4,6,720]{3,2,1,0:T(8,128)S(1)}, u32[]{:S(2)}, u32[]{:S(2)}) collective-permute-start(f32[5,4,6,720]{3,2,1,0:T(8,128)S(1)} %pad_maximum_fusion.29), channel_id=1, source_target_pairs={{0,2},{1,3},{2,0},{3,1},{4,6},{5,7},{6,4},{7,5},{8,10},{9,11},{10,... | collective-permute-start | bytes 1036808 | tf_op jit(solution)/shard_map/ppermute | solution.py:29
  148.7 12.9 %collective-permute-start.9 = (f32[28,14,3]{2,1,0:T(8,128)S(1)}, f32[28,14,3]{2,1,0:T(8,128)S(1)}, u32[]{:S(2)}, u32[]{:S(2)}) collective-permute-start(f32[28,14,3]{2,1,0:T(8,128)S(1)} %get-tuple-element.13), channel_id=1, source_target_pairs={{0,1},{1,2},{2,3},{3,0},{4,5},{5,6},{6,7},{7,4},{8,9},{9,10},{10,1... | collective-permute-start | bytes 14120 | tf_op jit(solution)/shard_map/ppermute | solution.py:18
  150.1 22.8 %collective-permute-start.10 = (f32[28,14,3]{2,1,0:T(8,128)S(1)}, f32[28,14,3]{2,1,0:T(8,128)S(1)}, u32[]{:S(2)}, u32[]{:S(2)}) collective-permute-start(f32[28,14,3]{2,1,0:T(8,128)S(1)} %get-tuple-element.14), channel_id=1, source_target_pairs={{1,0},{2,1},{3,2},{0,3},{5,4},{6,5},{7,6},{4,7},{9,8},{10,9},{11,1... | collective-permute-start | bytes 14120 | tf_op jit(solution)/shard_map/ppermute | solution.py:20
  153.3 8.4 %copy-start.16 = (f32[4,9,720]{2,1,0:T(8,128)}, f32[4,9,720]{2,1,0:T(8,128)S(1)}, u32[]{:S(2)}) copy-start(f32[4,9,720]{2,1,0:T(8,128)S(1)} %get-tuple-element.8) | copy-start | bytes 311044
  173.6 1.6 copy-start.2
  176.5 10.0 %copy-start.8 = (f32[5,4,8,720]{3,2,1,0:T(8,128)S(1)}, f32[5,4,8,720]{3,2,1,0:T(8,128)}, u32[]{:S(2)}) copy-start(f32[5,4,8,720]{3,2,1,0:T(8,128)} %slice.362) | copy-start | bytes 1382404
  186.7 0.9 copy-start.17
  186.7 1.0 copy-start.20
  186.7 1.1 copy-start.21
  187.8 1.0 copy-start.12
  188.9 1.6 copy-start.1
  193.7 68.5 %copy-start.15 = (f32[160,720]{1,0:T(8,128)S(1)}, f32[160,720]{1,0:T(8,128)}, u32[]{:S(2)}) copy-start(f32[160,720]{1,0:T(8,128)} %copy-done.14) | copy-start | bytes 1382404
  193.7 23.9 %collective-permute-start.12 = (f32[160,1440]{1,0:T(8,128)S(1)}, f32[160,1440]{1,0:T(8,128)S(1)}, u32[]{:S(2)}, u32[]{:S(2)}) collective-permute-start(f32[160,1440]{1,0:T(8,128)S(1)} %fusion.8), channel_id=1, source_target_pairs={{0,1},{1,0},{2,3},{3,2},{4,5},{5,4},{6,7},{7,6},{8,9},{9,8},{10,11... | collective-permute-start | bytes 2764808 | tf_op jit(solution)/shard_map/ppermute | solution.py:131
  217.8 44.4 %collective-permute-start.13 = (f32[160,1440]{1,0:T(8,128)S(1)}, f32[160,1440]{1,0:T(8,128)S(1)}, u32[]{:S(2)}, u32[]{:S(2)}) collective-permute-start(f32[160,1440]{1,0:T(8,128)S(1)} %add.188), channel_id=1, source_target_pairs={{0,2},{1,3},{2,0},{3,1},{4,6},{5,7},{6,4},{7,5},{8,10},{9,11},{10,... | collective-permute-start | bytes 2764808 | tf_op jit(solution)/shard_map/ppermute | solution.py:131
